TPU v7x, 512 devices: a whole 4x8x8 slice. The times are simulated.
512 devices in a mesh: dp: 16 (over y, x_lo), table: 32 (over z, x_hi, core).
Axes of the slice: x: 4 (x_hi: 2, x_lo: 2; x = x_hi * 2 + x_lo), y: 8, z: 8, core: 2. Of those that a mesh axis runs over, the one named last changes fastest.
Arguments:
- id_table: bfloat16 [32768, 256], P('table'), may hold values from -2 to 2
- lookup_ids: int32 [65536, 8, 2], P(('dp', 'table')), may hold values from 0 to 32767, as said below
- row_owner: int32 [32768], replicated, may hold values from 0 to 32767, as said below
- query_tower: bfloat16 [1024, 256], replicated, may hold values from -1 to 1
- item_tower: bfloat16 [1024, 256], replicated, may hold values from -1 to 1
- row_seeds: int32 [32768], P('table'), may hold values from 0 to 1073741823
- tower_seeds: int32 [2, 1024], replicated, may hold values from 0 to 1073741823
Outputs:
- table_update: float32 [32768, 256], P('table')
- tower_update: float32 [2, 1024, 256], replicated
Inputs may be any that keep to these rules, and one draw needn't show every extreme that they name: `lookup_ids`: in every aligned block of 128 examples (the examples of one device), at most 96 of the lookups have row_owner[id] // 1024 equal to any one table shard, and exactly 96 do for some shard. A permutation: the row of id i lies at position row_owner[i] of id_table, on table shard row_owner[i] // 1024.
All inputs are finite; a program needn't handle non-finite values.
Results may differ from a plain program's by a relative error of at most 0.0073.
The roundings to bfloat16 on the way count: a program that leaves them out, or rounds other values in their place, can miss the bound.
Values may be sent and summed in bfloat16 or wider, within the bound.
No kernel may reach another device: no remote copies, remote signals or barrier semaphores. Data moves between devices by JAX's collectives and lax.ppermute only.
A program may use at most 64 MiB of HBM per device.

v0:
```python
import math
import jax
import jax.numpy as jnp
from jax import lax
from jax.sharding import PartitionSpec as P

NOISE_MULT = 0.1


def hashed_noise(seed_rows, width):
    columns = jnp.arange(width, dtype=jnp.int32)
    summed = jnp.zeros(seed_rows.shape + (width,), jnp.float32)
    for section in range(2):
        mixed = seed_rows[..., None] + (columns * 2 + section) * 1013904223
        mixed = mixed ^ mixed >> 15 & 131071
        mixed = mixed * 73244475
        mixed = mixed ^ mixed >> 13 & 524287
        mixed = mixed * 1597334677
        mixed = mixed ^ mixed >> 16 & 65535
        lower = (mixed & 65535).astype(jnp.float32) / 65536.0 - 0.5
        upper = (mixed >> 16 & 65535).astype(jnp.float32) / 65536.0 - 0.5
        summed = summed + lower + upper
    return summed * math.sqrt(3.0)


def squares(values):
    return jnp.sum(jnp.square(values.astype(jnp.float32)), axis=1)


def body(id_table, lookup_ids, row_owner, query_tower, item_tower, row_seeds, tower_seeds):
    shards = lax.axis_size("table")
    rows_dev, emb_width = id_table.shape
    batch, slots, bags = lookup_ids.shape
    feats = slots // 2
    hidden_width, out_width = query_tower.shape
    scale = 200.0 / math.sqrt(out_width)
    clip_norm = 0.9 * math.sqrt(2.0 * hidden_width + 400.0)
    requests = batch * slots * bags
    capacity = 3 * requests // (2 * shards)
    positions = row_owner[lookup_ids.reshape(-1)]
    owners = positions // rows_dev
    local_rows = positions - owners * rows_dev
    one_hot = (owners[:, None] == jnp.arange(shards, dtype=jnp.int32)[None, :]).astype(jnp.int32)
    ranks = jnp.sum((jnp.cumsum(one_hot, axis=0) - one_hot) * one_hot, axis=1)
    targets = owners * capacity + ranks
    outgoing = jnp.full((shards * capacity,), -1, jnp.int32).at[targets].set(local_rows)
    outgoing = outgoing.reshape(shards, capacity)
    incoming = lax.all_to_all(outgoing, "table", split_axis=0, concat_axis=0, tiled=True)
    valid = incoming >= 0
    fetched = id_table[jnp.where(valid, incoming, 0)]
    fetched = jnp.where(valid[:, :, None], fetched, jnp.zeros((), jnp.bfloat16))
    returned = lax.all_to_all(fetched, "table", split_axis=0, concat_axis=0, tiled=True)
    returned, incoming = (returned, incoming)
    looked = returned.reshape(shards * capacity, emb_width)[targets]
    pooled = jnp.sum(looked.reshape(batch, slots, bags, emb_width).astype(jnp.float32), axis=2)
    pooled = pooled.astype(jnp.bfloat16)
    query_in = pooled[:, :feats].reshape(batch, hidden_width)
    item_in = pooled[:, feats:].reshape(batch, hidden_width)
    query_vec = jnp.dot(query_in, query_tower, preferred_element_type=jnp.float32).astype(
        jnp.bfloat16
    )
    item_vec = jnp.dot(item_in, item_tower, preferred_element_type=jnp.float32).astype(jnp.bfloat16)
    all_items = lax.all_gather(item_vec, "dp", axis=0, tiled=True)
    scores = scale * lax.dot_general(
        query_vec, all_items, (((1,), (1,)), ((), ())), preferred_element_type=jnp.float32
    )
    peak = jnp.max(scores, axis=1, keepdims=True)
    log_total = peak + jnp.log(jnp.sum(jnp.exp(scores - peak), axis=1, keepdims=True))
    probs = jnp.exp(scores - log_total).astype(jnp.bfloat16)
    query_grad = (
        scale
        * (
            jnp.dot(probs, all_items, preferred_element_type=jnp.float32)
            - item_vec.astype(jnp.float32)
        )
    ).astype(jnp.bfloat16)
    weighted = lax.psum_scatter(
        lax.dot_general(
            probs, query_vec, (((0,), (0,)), ((), ())), preferred_element_type=jnp.float32
        ),
        "dp",
        scatter_dimension=0,
        tiled=True,
    )
    item_grad = (scale * (weighted - query_vec.astype(jnp.float32))).astype(jnp.bfloat16)
    query_back = lax.dot_general(
        query_grad, query_tower, (((1,), (1,)), ((), ())), preferred_element_type=jnp.float32
    )
    item_back = lax.dot_general(
        item_grad, item_tower, (((1,), (1,)), ((), ())), preferred_element_type=jnp.float32
    )
    norm_sq = (
        squares(query_in) * squares(query_grad)
        + squares(item_in) * squares(item_grad)
        + squares(query_back)
        + squares(item_back)
    )
    factor = jnp.minimum(1.0, clip_norm / jnp.sqrt(norm_sq + 1e-06))
    clipped_query = (factor[:, None] * query_grad.astype(jnp.float32)).astype(jnp.bfloat16)
    clipped_item = (factor[:, None] * item_grad.astype(jnp.float32)).astype(jnp.bfloat16)
    tower_part = jnp.stack(
        [
            lax.dot_general(
                query_in,
                clipped_query,
                (((0,), (0,)), ((), ())),
                preferred_element_type=jnp.float32,
            ),
            lax.dot_general(
                item_in, clipped_item, (((0,), (0,)), ((), ())), preferred_element_type=jnp.float32
            ),
        ]
    )
    tower_sum = lax.psum(tower_part, ("dp", "table"))
    back_all = jnp.concatenate(
        [query_back.reshape(batch, feats, emb_width), item_back.reshape(batch, feats, emb_width)],
        axis=1,
    )
    lookup_grad = (factor[:, None, None] * back_all).astype(jnp.bfloat16)
    spread = jnp.broadcast_to(lookup_grad[:, :, None, :], (batch, slots, bags, emb_width))
    spread = spread.reshape(requests, emb_width)
    grad_out = jnp.zeros((shards * capacity, emb_width), jnp.bfloat16).at[targets].set(spread)
    grad_in = lax.all_to_all(
        grad_out.reshape(shards, capacity, emb_width),
        "table",
        split_axis=0,
        concat_axis=0,
        tiled=True,
    )
    flat_in = incoming.reshape(-1)
    slot_rows = jnp.where(flat_in >= 0, flat_in, rows_dev)
    row_sum = (
        jnp.zeros((rows_dev, emb_width), jnp.float32)
        .at[slot_rows]
        .add(grad_in.reshape(shards * capacity, emb_width).astype(jnp.float32), mode="drop")
    )
    row_count = (
        jnp.zeros((rows_dev,), jnp.float32)
        .at[slot_rows]
        .add((flat_in >= 0).astype(jnp.float32), mode="drop")
    )
    row_sum, row_count = lax.psum((row_sum, row_count), "dp")
    row_noise = hashed_noise(row_seeds, emb_width)
    table_update = row_sum / clip_norm + NOISE_MULT * jnp.where(
        row_count[:, None] > 0.0, row_noise, 0.0
    )
    tower_update = tower_sum / clip_norm + NOISE_MULT * hashed_noise(tower_seeds, out_width)
    return (table_update, tower_update)


def solution(mesh):
    in_specs = (P("table", None), P(("dp", "table"), None, None), P(), P(), P(), P("table"), P())
    out_specs = (P("table", None), P())
    return jax.shard_map(body, mesh=mesh, in_specs=in_specs, out_specs=out_specs, check_vma=False)
```

profile of v0, /device:TPU:4, one launch (start us, length us, event | category | flops | bytes accessed | tf_op | source)
XLA Modules:
  0.0 749.2 jit_solution(12677365749732896167)
XLA Ops:
  7.2 1.0 copy.37
  8.2 0.3 reshape.312
  8.6 11.8 %gather_fusion = s32[2048]{0:T(1024)S(1)} fusion(s32[32768]{0:T(1024)S(1)} %copy-done.1, s32[2048]{0:T(1024)S(1)} %broadcast_clamp_fusion.2), kind=kCustom, calls=%fused_computation | custom fusion | bytes 24576 | tf_op jit(solution)/shard_map/gather | solution.py:40
  20.4 9.1 %reduce-window.6 = s32[32,16,128]{2,1,0:T(8,128)S(1)} reduce-window(s32[32,16,128]{2,1,0:T(8,128)S(1)} %fusion.35, s32[]{:T(128)} %constant.35.clone.1), window={size=1x1x128 pad=0_0x0_0x127_0}, to_apply=%region_0.1 | reduce-window | flops 8323072 | bytes 524292 | tf_op jit(solution)/shard_map/reduce-window
  29.6 0.2 copy.45
  30.4 8.1 %scatter_custom_fusion = s32[3072]{0:T(1024)S(1)} fusion(s32[2048]{0:T(1024)S(1)} %bitcast.90, s32[2048]{0:T(1024)S(1)} %get-tuple-element.8, s32[]{:T(128)} %constant.34.clone.1), kind=kCustom, calls=%fused_computation.112 | custom fusion | bytes 12292 | tf_op jit(solution)/shard_map/scatter | solution.py:46
  38.6 20.4 %all_to_all.22 = s32[32,1,96]{2,1,0:T(1,128)S(1)} all-to-all(s32[32,1,96]{2,1,0:T(1,128)S(1)} %all_to_all.14), channel_id=1, replica_groups=mesh['dp'=16,'table'=32] {'table'}, dimensions={0} | all-to-all | bytes 24576 | tf_op jit(solution)/shard_map/all_to_all | solution.py:48
  59.0 0.6 fusion.54
  59.7 11.1 %gather_fusion.1 = bf16[3072,256]{1,0:T(8,128)(2,1)S(1)} fusion(bf16[1024,256]{1,0:T(8,128)(2,1)S(1)} %copy-done, s32[3072]{0:T(1024)S(1)} %broadcast_clamp_fusion), kind=kCustom, calls=%fused_computation.1 | custom fusion | bytes 3158016 | tf_op jit(solution)/shard_map/gather | solution.py:50
  70.7 1.5 broadcast_select_fusion
  72.2 6.4 all-to-all-start.1
  78.7 39.2 %all-to-all-done.1 = bf16[32,96,256]{2,1,0:T(8,128)(2,1)S(1)} async-done(((bf16[32,96,256]{2,1,0:T(8,128)(2,1)}), bf16[32,96,256]{2,1,0:T(8,128)(2,1)S(1)}, u32[]{:S(2)}, u32[]{:S(2)}) %all-to-all-start.1) | async-done | bytes 1572896 | tf_op jit(solution)/shard_map/all_to_all | solution.py:52
  117.9 7.5 gather_fusion.2
  125.4 0.4 reshape.316
  125.9 2.8 reduce_sum.88
  128.9 0.2 copy.44
  129.2 0.9 convolution_convert_fusion
  130.5 0.3 convolution_convert_fusion.1
  130.8 67.7 %all-gather.2.cloned.1.call-done = bf16[2048,256]{1,0:T(8,128)(2,1)} async-done(((bf16[128,256]{1,0:T(8,128)(2,1)}), bf16[2048,256]{1,0:T(8,128)(2,1)}) %all-gather.2.cloned.1.call-update) | async-done | bytes 1048592 | tf_op jit(solution)/shard_map/all_gather | solution.py:63
  198.5 1.8 fusion.56
  200.3 0.3 exponential_reduce_fusion
  200.6 1.9 fusion.53
  202.6 1.8 multiply_reduce_fusion.2
  204.4 1.8 fusion.36
  206.2 0.4 multiply_reduce_fusion.1
  206.6 0.3 concatenate.11
  206.9 73.6 %reduce-scatter.2.cloned.1.call-done = f32[128,256]{1,0:T(8,128)} async-done(((f32[2048,256]{1,0:T(8,128)}), f32[128,256]{1,0:T(8,128)}) %reduce-scatter.2.cloned.1.call-update) | async-done | bytes 131088 | tf_op jit(solution)/shard_map/reduce_scatter | solution.py:77
  280.5 1.0 fusion.38
  281.5 0.4 multiply_reduce_fusion
  281.9 0.3 concatenate.12
  282.2 0.2 fusion.28
  282.5 0.7 broadcast_in_dim.40
  283.2 0.4 reshape.359
  283.7 10.7 %scatter_custom_fusion.1 = bf16[3072,256]{1,0:T(8,128)(2,1)} fusion(s32[2048]{0:T(1024)} %bitcast.92, bf16[2048,256]{1,0:T(8,128)(2,1)S(1)} %reshape.359, bf16[]{:T(256)} %constant.43.clone.1), kind=kCustom, calls=%fused_computation.57 | custom fusion | bytes 1573376 | tf_op jit(solution)/shard_map/scatter | solution.py:122
  294.4 10.3 %all-to-all-start.2 = ((bf16[32,96,256]{2,1,0:T(8,128)(2,1)}), bf16[32,96,256]{2,1,0:T(8,128)(2,1)S(1)}, u32[]{:S(2)}, u32[]{:S(2)}) async-start(bf16[32,96,256]{2,1,0:T(8,128)(2,1)} %bitcast.77), calls=%async_computation.3 | async-start | bytes 3145728 | tf_op jit(solution)/shard_map/all_to_all | solution.py:123
  304.7 0.3 convolution_bitcast_fusion
  305.1 0.3 convolution_bitcast_fusion.1
  305.4 1.5 pad_maximum_fusion
  307.0 0.5 broadcast.460
  307.5 0.7 reduce.6
  308.3 37.0 %all-to-all-done.2 = bf16[32,96,256]{2,1,0:T(8,128)(2,1)S(1)} async-done(((bf16[32,96,256]{2,1,0:T(8,128)(2,1)}), bf16[32,96,256]{2,1,0:T(8,128)(2,1)S(1)}, u32[]{:S(2)}, u32[]{:S(2)}) %all-to-all-start.2) | async-done | bytes 1572896 | tf_op jit(solution)/shard_map/all_to_all | solution.py:123
  345.3 18.1 %scatter_custom_fusion.2 = f32[1024,256]{1,0:T(8,128)} fusion(s32[3072]{0:T(1024)S(1)} %bitcast.95, bf16[3072,256]{1,0:T(8,128)(2,1)S(1)} %bitcast.76, f32[]{:T(128)} %constant.33.clone.1), kind=kCustom, calls=%fused_computation.7 | custom fusion | flops 1572864 | bytes 2621444 | tf_op jit(solution)/shard_map/scatter-add | solution.py:135
  363.5 19.7 %scatter_custom_fusion.3 = f32[1024]{0:T(1024)S(1)} fusion(s32[3072]{0:T(1024)S(1)} %bitcast.96, f32[3072]{0:T(1024)S(1)} %reshape.375, f32[]{:T(128)} %constant.33.clone.1), kind=kCustom, calls=%fused_computation.117 | custom fusion | flops 3072 | bytes 4100 | tf_op jit(solution)/shard_map/scatter-add | solution.py:140
  383.2 32.3 %psum.22 = f32[1024]{0:T(1024)S(1)} all-reduce(f32[1024]{0:T(1024)S(1)} %scatter_custom_fusion.3), channel_id=1, replica_groups=mesh['dp'=16,'table'=32] {'dp'}, use_global_device_ids=true, to_apply=%region_18.19 | all-reduce | flops 1024 | bytes 8192 | tf_op jit(solution)/shard_map/psum | solution.py:142
  415.5 177.9 %all-reduce.5.cloned.1.call-done = f32[2,1024,256]{2,1,0:T(8,128)} async-done(((f32[2,1024,256]{2,1,0:T(8,128)}), f32[2,1024,256]{2,1,0:T(8,128)}) %all-reduce.5.cloned.1.call-update) | async-done | bytes 2097168 | tf_op jit(solution)/shard_map/psum | solution.py:114
  593.4 5.3 multiply_add_fusion
  598.7 140.4 %all-reduce.3.cloned.1.call-done = f32[1024,256]{1,0:T(8,128)} async-done(((f32[1024,256]{1,0:T(8,128)}), f32[1024,256]{1,0:T(8,128)}) %all-reduce.3.cloned.1.call-update) | async-done | bytes 1048592 | tf_op jit(solution)/shard_map/psum | solution.py:142
  739.2 3.5 multiply_add_fusion.1
  (64 shorter events, 2.0 us)
Async XLA Ops:
  7.2 52.5 %copy-start = (bf16[1024,256]{1,0:T(8,128)(2,1)S(1)}, bf16[1024,256]{1,0:T(8,128)(2,1)}, u32[]{:S(2)}) copy-start(bf16[1024,256]{1,0:T(8,128)(2,1)} %param.7) | copy-start | bytes 1572868
  7.2 1.4 copy-start.1
  30.4 48.3 %copy-start.9 = (s32[2048,1]{0,1:T(1,128)}, s32[2048,1]{0,1:T(1,128)S(1)}, u32[]{:S(2)}) copy-start(s32[2048,1]{0,1:T(1,128)S(1)} %compare_select_fusion.2) | copy-start | bytes 24580
  72.2 45.7 %all-to-all-start.1 = ((bf16[32,96,256]{2,1,0:T(8,128)(2,1)}), bf16[32,96,256]{2,1,0:T(8,128)(2,1)S(1)}, u32[]{:S(2)}, u32[]{:S(2)}) async-start(bf16[32,96,256]{2,1,0:T(8,128)(2,1)} %broadcast_select_fusion), calls=%async_computation.1 | async-start | bytes 3145728 | tf_op jit(solution)/shard_map/all_to_all | solution.py:52
  78.6 119.9 %all-gather.2.cloned.1.call-start = ((), (), s32[]{:S(2)}) async-start(), calls=%async_computation.4 | async-start | bytes 1114112 | tf_op jit(solution)/shard_map/all_gather | solution.py:63
  125.8 3.3 copy-start.6
  125.8 4.7 copy-start.4
  128.9 1.9 copy-start.3
  130.1 150.4 %reduce-scatter.2.cloned.1.call-start = ((), (), s32[]{:S(2)}) async-start(), calls=%async_computation.5 | async-start | bytes 2228224 | tf_op jit(solution)/shard_map/reduce_scatter | solution.py:77
  200.6 1.9 copy-start.15
  202.5 1.9 copy-start.2
  202.5 3.7 copy-start.5
  206.2 75.3 %copy-start.7 = (bf16[1024,256]{1,0:T(8,128)(2,1)S(1)}, bf16[1024,256]{1,0:T(8,128)(2,1)}, u32[]{:S(2)}) copy-start(bf16[1024,256]{1,0:T(8,128)(2,1)} %param.11) | copy-start | bytes 1572868
  206.2 76.0 %copy-start.12 = (f32[128]{0:T(128)S(1)}, f32[128]{0:T(128)}, u32[]{:S(2)}) copy-start(f32[128]{0:T(128)} %get-tuple-element.18) | copy-start | bytes 1540
  206.2 76.0 %copy-start.13 = (f32[128]{0:T(128)S(1)}, f32[128]{0:T(128)}, u32[]{:S(2)}) copy-start(f32[128]{0:T(128)} %get-tuple-element.19) | copy-start | bytes 1540
  206.2 76.0 %copy-start.14 = (f32[128]{0:T(128)S(1)}, f32[128]{0:T(128)}, u32[]{:S(2)}) copy-start(f32[128]{0:T(128)} %get-tuple-element.16) | copy-start | bytes 1540
  294.4 50.9 %all-to-all-start.2 = ((bf16[32,96,256]{2,1,0:T(8,128)(2,1)}), bf16[32,96,256]{2,1,0:T(8,128)(2,1)S(1)}, u32[]{:S(2)}, u32[]{:S(2)}) async-start(bf16[32,96,256]{2,1,0:T(8,128)(2,1)} %bitcast.77), calls=%async_computation.3 | async-start | bytes 3145728 | tf_op jit(solution)/shard_map/all_to_all | solution.py:123
  304.7 288.7 %all-reduce.5.cloned.1.call-start = ((), (), s32[]{:S(2)}) async-start(), calls=%async_computation.7 | async-start | bytes 4194304 | tf_op jit(solution)/shard_map/psum | solution.py:114
  306.9 56.6 %copy-start.8 = (f32[32,1,96]{2,0,1:T(8,128)S(1)}, f32[32,1,96]{2,0,1:T(8,128)}, u32[]{:S(2)}) copy-start(f32[32,1,96]{2,0,1:T(8,128)} %get-tuple-element.2) | copy-start | bytes 36868
  306.9 286.5 %copy-start.10 = (s32[2,1024]{1,0:T(2,128)S(1)}, s32[2,1024]{1,0:T(2,128)}, u32[]{:S(2)}) copy-start(s32[2,1024]{1,0:T(2,128)} %param.13) | copy-start | bytes 24580
  306.9 432.2 %all-reduce.3.cloned.1.call-start = ((), (), s32[]{:S(2)}) async-start(), calls=%async_computation.6 | async-start | bytes 2097152 | tf_op jit(solution)/shard_map/psum | solution.py:142
  593.4 145.7 %copy-start.11 = (s32[1024]{0:T(1024)S(1)}, s32[1024]{0:T(1024)}, u32[]{:S(2)}) copy-start(s32[1024]{0:T(1024)} %param.12) | copy-start | bytes 12292
Sparse Core Ops, SparseCore 0:
  130.2 68.2 all-gather.1
  202.7 77.8 reduce-scatter.1
  311.0 282.3 all-reduce.4
  597.0 142.0 all-reduce.2
where the time goes:
time: 750 us; the launch traced here: 749 us
  waiting for transfers between devices  536 us (71%)
  other arithmetic  66.8 us (9%)
  local copies, waits for them, and re-layouts  54.5 us (7%)
  blocking collectives  52.7 us (7%)
  starting transfers between devices  17.1 us (2%)
  between operations  14.2 us (2%)
  matrix products  8.08 us (1%)
    psum x1, waiting for transfers between devices, body(): tower_sum = lax.psum(tower_part, ('dp', 'table'))  178 us
    psum x1, waiting for transfers between devices, body(): row_sum, row_count = lax.psum((row_sum, row_count), 'dp')  140 us
    reduce_scatter x1, waiting for transfers between devices, body(): lax.psum_scatter(lax.dot_general(probs, query_vec, (((0,), (0,)), ((), ()...  73.6 us
    all_gather x1, waiting for transfers between devices, body(): all_items = lax.all_gather(item_vec, 'dp', axis=0, tiled=True)  67.7 us
    all_to_all x1, waiting for transfers between devices, body(): lax.all_to_all(fetched, 'table', split_axis=0, concat_axis=0, tiled=True)  39.2 us
    all_to_all x1, waiting for transfers between devices, body(): lax.all_to_all(grad_out.reshape(shards, capacity, emb_width), 'table', sp...  37 us
    psum x1, blocking collectives, body(): row_sum, row_count = lax.psum((row_sum, row_count), 'dp')  32.3 us
    all_to_all x1, blocking collectives, body(): lax.all_to_all(outgoing, 'table', split_axis=0, concat_axis=0, tiled=True)  20.4 us
  transfers between devices with their start and end apart: 6, of which 6 were waited for; matrix products, arithmetic and copies ran while one was open for 7% of the time, Pallas kernels for 0%

commit v1 on v0

--- a/solution.py
+++ b/solution.py
@@ -3,6 +3,7 @@
 import jax.numpy as jnp
 from jax import lax
 from jax.sharding import PartitionSpec as P
+from jax.lax import psum
 
 NOISE_MULT = 0.1
 
@@ -111,7 +112,9 @@
             ),
         ]
     )
-    tower_sum = lax.psum(tower_part, ("dp", "table"))
+    tower_sum = tower_part
+    for idx in ("dp", "table"):
+        tower_sum = psum(tower_sum, idx)
     back_all = jnp.concatenate(
         [query_back.reshape(batch, feats, emb_width), item_back.reshape(batch, feats, emb_width)],
         axis=1,

time: 750 us -> 821 us (1.095)
  the two profiles are of different devices: /device:TPU:4 before, /device:TPU:1 now
where the time goes in v1:
time: 821 us; the launch traced here: 820 us
  waiting for transfers between devices  601 us (73%)
  other arithmetic  65.8 us (8%)
  local copies, waits for them, and re-layouts  54.5 us (7%)
  blocking collectives  50.4 us (6%)
  starting transfers between devices  26 us (3%)
  between operations  14.2 us (2%)
    psum x1, waiting for transfers between devices, body(): tower_sum = psum(tower_sum, idx)  234 us
    psum x1, waiting for transfers between devices, body(): row_sum, row_count = lax.psum((row_sum, row_count), 'dp')  162 us
    reduce_scatter x1, waiting for transfers between devices, body(): lax.psum_scatter(lax.dot_general(probs, query_vec, (((0,), (0,)), ((), ()...  72.4 us
    all_gather x1, waiting for transfers between devices, body(): all_items = lax.all_gather(item_vec, 'dp', axis=0, tiled=True)  58 us
    all_to_all x1, waiting for transfers between devices, body(): lax.all_to_all(fetched, 'table', split_axis=0, concat_axis=0, tiled=True)  39.1 us
    all_to_all x1, waiting for transfers between devices, body(): lax.all_to_all(grad_out.reshape(shards, capacity, emb_width), 'table', sp...  35.6 us
    psum x1, blocking collectives, body(): row_sum, row_count = lax.psum((row_sum, row_count), 'dp')  26.8 us
    all_to_all x1, blocking collectives, body(): lax.all_to_all(outgoing, 'table', split_axis=0, concat_axis=0, tiled=True)  23.6 us
  transfers between devices with their start and end apart: 6, of which 6 were waited for; matrix products, arithmetic and copies ran while one was open for 4% of the time, Pallas kernels for 0%

profile of v1, /device:TPU:1, one launch (start us, length us, event | category | flops | bytes accessed | tf_op | source)
XLA Modules:
  0.0 820.1 jit_solution(12416371590583594255)
XLA Ops:
  7.2 1.0 copy.37
  8.2 0.3 reshape.312
  8.6 11.8 %gather_fusion = s32[2048]{0:T(1024)S(1)} fusion(s32[32768]{0:T(1024)S(1)} %copy-done.1, s32[2048]{0:T(1024)S(1)} %broadcast_clamp_fusion.2), kind=kCustom, calls=%fused_computation | custom fusion | bytes 24576 | tf_op jit(solution)/shard_map/gather | solution.py:41
  20.4 9.1 %reduce-window.6 = s32[32,16,128]{2,1,0:T(8,128)S(1)} reduce-window(s32[32,16,128]{2,1,0:T(8,128)S(1)} %fusion.35, s32[]{:T(128)} %constant.35.clone.1), window={size=1x1x128 pad=0_0x0_0x127_0}, to_apply=%region_0.1 | reduce-window | flops 8323072 | bytes 524292 | tf_op jit(solution)/shard_map/reduce-window
  29.6 0.2 copy.45
  30.4 8.1 scatter_custom_fusion
  38.6 23.6 %all_to_all.22 = s32[32,1,96]{2,1,0:T(1,128)S(1)} all-to-all(s32[32,1,96]{2,1,0:T(1,128)S(1)} %all_to_all.14), channel_id=1, replica_groups=mesh['dp'=16,'table'=32] {'table'}, dimensions={0} | all-to-all | bytes 24576 | tf_op jit(solution)/shard_map/all_to_all | solution.py:49
  62.2 0.6 fusion.54
  62.9 11.1 %gather_fusion.1 = bf16[3072,256]{1,0:T(8,128)(2,1)S(1)} fusion(bf16[1024,256]{1,0:T(8,128)(2,1)S(1)} %copy-done, s32[3072]{0:T(1024)S(1)} %broadcast_clamp_fusion), kind=kCustom, calls=%fused_computation.1 | custom fusion | bytes 3158016 | tf_op jit(solution)/shard_map/gather | solution.py:51
  73.9 1.5 broadcast_select_fusion
  75.4 4.2 all-to-all-start.1
  79.7 39.1 %all-to-all-done.1 = bf16[32,96,256]{2,1,0:T(8,128)(2,1)S(1)} async-done(((bf16[32,96,256]{2,1,0:T(8,128)(2,1)}), bf16[32,96,256]{2,1,0:T(8,128)(2,1)S(1)}, u32[]{:S(2)}, u32[]{:S(2)}) %all-to-all-start.1) | async-done | bytes 1572896 | tf_op jit(solution)/shard_map/all_to_all | solution.py:53
  118.8 7.5 gather_fusion.2
  126.3 0.4 reshape.316
  126.8 2.8 reduce_sum.88
  129.8 0.2 copy.44
  130.1 0.9 convolution_convert_fusion
  131.4 0.3 convolution_convert_fusion.1
  131.7 58.0 %all-gather.2.cloned.1.call-done = bf16[2048,256]{1,0:T(8,128)(2,1)} async-done(((bf16[128,256]{1,0:T(8,128)(2,1)}), bf16[2048,256]{1,0:T(8,128)(2,1)}) %all-gather.2.cloned.1.call-update) | async-done | bytes 1048592 | tf_op jit(solution)/shard_map/all_gather | solution.py:64
  189.7 1.8 fusion.56
  191.5 0.3 exponential_reduce_fusion
  191.8 1.9 fusion.53
  193.8 1.8 multiply_reduce_fusion.2
  195.6 1.8 fusion.36
  197.4 0.4 multiply_reduce_fusion.1
  197.8 0.3 concatenate.11
  198.1 72.4 %reduce-scatter.2.cloned.1.call-done = f32[128,256]{1,0:T(8,128)} async-done(((f32[2048,256]{1,0:T(8,128)}), f32[128,256]{1,0:T(8,128)}) %reduce-scatter.2.cloned.1.call-update) | async-done | bytes 131088 | tf_op jit(solution)/shard_map/reduce_scatter | solution.py:78
  270.5 1.0 fusion.38
  271.5 0.4 multiply_reduce_fusion
  271.9 0.3 concatenate.12
  272.2 0.2 fusion.28
  272.5 0.7 broadcast_in_dim.40
  273.2 0.4 reshape.359
  273.6 10.7 %scatter_custom_fusion.1 = bf16[3072,256]{1,0:T(8,128)(2,1)} fusion(s32[2048]{0:T(1024)} %bitcast.92, bf16[2048,256]{1,0:T(8,128)(2,1)S(1)} %reshape.359, bf16[]{:T(256)} %constant.43.clone.1), kind=kCustom, calls=%fused_computation.57 | custom fusion | bytes 1573376 | tf_op jit(solution)/shard_map/scatter | solution.py:125
  284.4 21.4 %all-to-all-start.2 = ((bf16[32,96,256]{2,1,0:T(8,128)(2,1)}), bf16[32,96,256]{2,1,0:T(8,128)(2,1)S(1)}, u32[]{:S(2)}, u32[]{:S(2)}) async-start(bf16[32,96,256]{2,1,0:T(8,128)(2,1)} %bitcast.77), calls=%async_computation.3 | async-start | bytes 3145728 | tf_op jit(solution)/shard_map/all_to_all | solution.py:126
  305.8 0.5 broadcast.460
  306.3 0.7 reduce.6
  307.1 0.3 convolution_bitcast_fusion
  307.5 0.4 convolution_bitcast_fusion.1
  307.9 1.5 pad_maximum_fusion
  309.3 35.6 %all-to-all-done.2 = bf16[32,96,256]{2,1,0:T(8,128)(2,1)S(1)} async-done(((bf16[32,96,256]{2,1,0:T(8,128)(2,1)}), bf16[32,96,256]{2,1,0:T(8,128)(2,1)S(1)}, u32[]{:S(2)}, u32[]{:S(2)}) %all-to-all-start.2) | async-done | bytes 1572896 | tf_op jit(solution)/shard_map/all_to_all | solution.py:126
  345.0 18.1 %scatter_custom_fusion.2 = f32[1024,256]{1,0:T(8,128)} fusion(s32[3072]{0:T(1024)S(1)} %bitcast.95, bf16[3072,256]{1,0:T(8,128)(2,1)S(1)} %bitcast.76, f32[]{:T(128)} %constant.33.clone.1), kind=kCustom, calls=%fused_computation.7 | custom fusion | flops 1572864 | bytes 2621444 | tf_op jit(solution)/shard_map/scatter-add | solution.py:138
  363.2 161.5 %all-reduce.6.cloned.1.call-done = (f32[1024,256]{1,0:T(8,128)}, f32[2,1024,256]{2,1,0:T(8,128)}) async-done(((f32[1024,256]{1,0:T(8,128)}, f32[2,1024,256]{2,1,0:T(8,128)}), (f32[1024,256]{1,0:T(8,128)}, f32[2,1024,256]{2,1,0:T(8,128)})) %all-reduce.6.cloned.1.call-update) | async-done | bytes 3145744 | tf_op jit(solution)/shard_map/psum | solution.py:145
  524.8 19.7 %scatter_custom_fusion.3 = f32[1024]{0:T(1024)S(1)} fusion(s32[3072]{0:T(1024)S(1)} %bitcast.96, f32[3072]{0:T(1024)S(1)} %reshape.375, f32[]{:T(128)} %constant.33.clone.1), kind=kCustom, calls=%fused_computation.117 | custom fusion | flops 3072 | bytes 4100 | tf_op jit(solution)/shard_map/scatter-add | solution.py:143
  544.5 26.8 %psum.29 = f32[1024]{0:T(1024)S(1)} all-reduce(f32[1024]{0:T(1024)S(1)} %scatter_custom_fusion.3), channel_id=1, replica_groups=mesh['dp'=16,'table'=32] {'dp'}, use_global_device_ids=true, to_apply=%region_18.19 | all-reduce | flops 1024 | bytes 8192 | tf_op jit(solution)/shard_map/psum | solution.py:145
  571.4 2.5 multiply_add_fusion.1
  573.9 234.4 %all-reduce.4.cloned.1.call-done = f32[2,1024,256]{2,1,0:T(8,128)} async-done(((f32[2,1024,256]{2,1,0:T(8,128)}), f32[2,1024,256]{2,1,0:T(8,128)}) %all-reduce.4.cloned.1.call-update) | async-done | bytes 2097168 | tf_op jit(solution)/shard_map/psum | solution.py:117
  808.3 5.3 multiply_add_fusion
  (66 shorter events, 2.0 us)
Async XLA Ops:
  7.2 55.7 %copy-start = (bf16[1024,256]{1,0:T(8,128)(2,1)S(1)}, bf16[1024,256]{1,0:T(8,128)(2,1)}, u32[]{:S(2)}) copy-start(bf16[1024,256]{1,0:T(8,128)(2,1)} %param.7) | copy-start | bytes 1572868
  7.2 1.4 copy-start.1
  30.4 49.3 %copy-start.10 = (s32[2048,1]{0,1:T(1,128)}, s32[2048,1]{0,1:T(1,128)S(1)}, u32[]{:S(2)}) copy-start(s32[2048,1]{0,1:T(1,128)S(1)} %compare_select_fusion.2) | copy-start | bytes 24580
  75.4 43.4 %all-to-all-start.1 = ((bf16[32,96,256]{2,1,0:T(8,128)(2,1)}), bf16[32,96,256]{2,1,0:T(8,128)(2,1)S(1)}, u32[]{:S(2)}, u32[]{:S(2)}) async-start(bf16[32,96,256]{2,1,0:T(8,128)(2,1)} %broadcast_select_fusion), calls=%async_computation.1 | async-start | bytes 3145728 | tf_op jit(solution)/shard_map/all_to_all | solution.py:53
  79.6 110.1 %all-gather.2.cloned.1.call-start = ((), (), s32[]{:S(2)}) async-start(), calls=%async_computation.4 | async-start | bytes 1114112 | tf_op jit(solution)/shard_map/all_gather | solution.py:64
  126.7 3.3 copy-start.6
  126.8 4.7 copy-start.4
  129.8 1.9 copy-start.3
  131.0 139.5 %reduce-scatter.2.cloned.1.call-start = ((), (), s32[]{:S(2)}) async-start(), calls=%async_computation.5 | async-start | bytes 2228224 | tf_op jit(solution)/shard_map/reduce_scatter | solution.py:78
  191.8 1.9 copy-start.16
  193.7 1.9 copy-start.2
  193.7 3.7 copy-start.5
  197.4 74.1 %copy-start.7 = (bf16[1024,256]{1,0:T(8,128)(2,1)S(1)}, bf16[1024,256]{1,0:T(8,128)(2,1)}, u32[]{:S(2)}) copy-start(bf16[1024,256]{1,0:T(8,128)(2,1)} %param.11) | copy-start | bytes 1572868
  197.4 74.8 %copy-start.13 = (f32[128]{0:T(128)S(1)}, f32[128]{0:T(128)}, u32[]{:S(2)}) copy-start(f32[128]{0:T(128)} %get-tuple-element.20) | copy-start | bytes 1540
  197.4 74.8 %copy-start.14 = (f32[128]{0:T(128)S(1)}, f32[128]{0:T(128)}, u32[]{:S(2)}) copy-start(f32[128]{0:T(128)} %get-tuple-element.21) | copy-start | bytes 1540
  197.4 74.8 %copy-start.15 = (f32[128]{0:T(128)S(1)}, f32[128]{0:T(128)}, u32[]{:S(2)}) copy-start(f32[128]{0:T(128)} %get-tuple-element.18) | copy-start | bytes 1540
  284.4 60.6 %all-to-all-start.2 = ((bf16[32,96,256]{2,1,0:T(8,128)(2,1)}), bf16[32,96,256]{2,1,0:T(8,128)(2,1)S(1)}, u32[]{:S(2)}, u32[]{:S(2)}) async-start(bf16[32,96,256]{2,1,0:T(8,128)(2,1)} %bitcast.77), calls=%async_computation.3 | async-start | bytes 3145728 | tf_op jit(solution)/shard_map/all_to_all | solution.py:126
  305.8 218.9 %all-reduce.6.cloned.1.call-start = ((), (), s32[]{:S(2)}) async-start(), calls=%async_computation.7 | async-start | bytes 6291456 | tf_op jit(solution)/shard_map/psum | solution.py:145
  363.1 161.6 %copy-start.9 = (f32[32,1,96]{2,0,1:T(8,128)S(1)}, f32[32,1,96]{2,0,1:T(8,128)}, u32[]{:S(2)}) copy-start(f32[32,1,96]{2,0,1:T(8,128)} %get-tuple-element.4) | copy-start | bytes 36868
  363.1 208.3 %copy-start.12 = (s32[1024]{0:T(1024)S(1)}, s32[1024]{0:T(1024)}, u32[]{:S(2)}) copy-start(s32[1024]{0:T(1024)} %param.12) | copy-start | bytes 12292
  363.1 445.2 %all-reduce.4.cloned.1.call-start = ((), (), s32[]{:S(2)}) async-start(), calls=%async_computation.6 | async-start | bytes 4194304 | tf_op jit(solution)/shard_map/psum | solution.py:117
  524.7 46.7 %copy-start.8 = (f32[1024,256]{1,0:T(8,128)S(1)}, f32[1024,256]{1,0:T(8,128)}, u32[]{:S(2)}) copy-start(f32[1024,256]{1,0:T(8,128)} %get-tuple-element.2) | copy-start | bytes 3145732
  524.7 283.6 %copy-start.11 = (s32[2,1024]{1,0:T(2,128)S(1)}, s32[2,1024]{1,0:T(2,128)}, u32[]{:S(2)}) copy-start(s32[2,1024]{1,0:T(2,128)} %param.13) | copy-start | bytes 24580
Sparse Core Ops, SparseCore 0:
  131.1 58.5 all-gather.1
  193.9 76.5 reduce-scatter.1
  363.2 161.3 all-reduce.5
  527.4 280.8 all-reduce.3
